TPU v7x, 128 devices: a whole 4x4x4 slice. The times are simulated.
128 devices in a mesh: expo: 8 (over z, core), sky: 16 (over x, y).
Axes of the slice: x: 4, y: 4, z: 4, core: 2. Of those that a mesh axis runs over, the one named last changes fastest.
Arguments:
- samples: bfloat16 [1024, 32, 256], P('sky'), may hold values from -0.75 to 0.75
- basis: bfloat16 [256, 1024], replicated, may hold values from -3 to 3
- operators: bfloat16 [1024, 1024, 1024], P(('expo', 'sky')), may hold values from -0.1875 to 0.1875
- cutouts: float32 [1024, 16, 1024], P(('expo', 'sky')), may hold values from -6 to 6
- pixel_weights: float32 [1024, 16, 1024], P(('expo', 'sky')), may hold values from 0.25 to 4
- detections: int32 [8, 16, 16, 12], P('expo', 'sky'), may hold values from -1 to 63, as said below
- intersections: int32 [1024, 16], P(('expo', 'sky')), may hold values from -1 to 191, as said below
Outputs:
- loglik: float32 [1024, 32], P('sky', 'expo')
- coeff_grads: float32 [1024, 32, 256], P('sky', 'expo')
Inputs may be any that keep to these rules, and one draw needn't show every extreme that they name: In detections[e, s, c], the live slots (values 0 or more) come first; -1 marks the rest. For every device (e, c), the live slots over all s total exactly 96, and one s fills all 12. A galaxy may stand in several slots. `intersections`: on device (e, c), a slot r = s * 12 + j is live exactly when detections[e, s, c, j] >= 0, and each live slot stands at exactly one position of the device's tiles; -1 marks empty positions. One tile of every device has all 16 positions filled.
All inputs are finite; a program needn't handle non-finite values.
Results may differ from a plain program's by a relative error of at most 0.0017.
Values may be sent and summed in bfloat16 or wider, within the bound.
No kernel may reach another device: no remote copies, remote signals or barrier semaphores. Data moves between devices by JAX's collectives and lax.ppermute only.
A program may use at most 128 MiB of HBM per device.

v0:
```python
import jax
import jax.numpy as jnp
from jax import lax
from jax.sharding import PartitionSpec as P


def galaxy_sums(listed, values, galaxy_count):
    flat_list = listed.reshape(-1)
    onehot = (flat_list[None, :] == jnp.arange(galaxy_count, dtype=jnp.int32)[:, None]).astype(
        jnp.float32
    )
    return jnp.dot(onehot, values.reshape(flat_list.shape[0], -1), precision=lax.Precision.HIGHEST)


def per_device(samples, basis, operators, cutouts, pixel_weights, detections, intersections):
    tiles_here, tile_cap, pixels = cutouts.shape
    coeff_dim = basis.shape[0]
    galaxy_count, sample_count, _unused = samples.shape
    sky_count = lax.axis_size("sky")
    send_cap = detections.shape[3]
    slot_count = sky_count * send_cap
    sent_rows = detections.reshape(sky_count, send_cap)
    flat_samples = samples.reshape(galaxy_count, sample_count * coeff_dim)
    outgoing = jnp.take(flat_samples, jnp.maximum(sent_rows, 0), axis=0)
    incoming = lax.all_to_all(outgoing, "sky", split_axis=0, concat_axis=0, tiled=True)
    incoming = incoming.reshape(slot_count, sample_count * coeff_dim)
    live = intersections >= 0
    picked = jnp.take(incoming, jnp.maximum(intersections, 0), axis=0).reshape(-1, coeff_dim)
    rendered = jnp.dot(picked, basis, preferred_element_type=jnp.float32).astype(jnp.bfloat16)
    rendered = rendered.reshape(tiles_here, tile_cap * sample_count, pixels)
    model = jnp.einsum("tnp,tpq->tnq", rendered, operators, preferred_element_type=jnp.float32)
    model = model.reshape(tiles_here, tile_cap, sample_count, pixels)
    resid = model - cutouts[:, :, None, :]
    weighted = pixel_weights[:, :, None, :] * resid
    pair_like = -0.5 / pixels * jnp.sum(weighted * resid, axis=-1)
    scaled = weighted.astype(jnp.bfloat16).reshape(tiles_here, tile_cap * sample_count, pixels)
    backed = jnp.einsum(
        "tnq,tpq->tnp", scaled, operators, preferred_element_type=jnp.float32
    ).astype(jnp.bfloat16)
    pair_grad = (
        -1.0
        / pixels
        * lax.dot_general(
            backed.reshape(-1, pixels),
            basis,
            (((1,), (1,)), ((), ())),
            preferred_element_type=jnp.float32,
        )
    )
    target = jnp.where(live, intersections, slot_count).reshape(-1)
    slot_grads = jnp.zeros((slot_count, sample_count * coeff_dim), jnp.float32)
    slot_grads = slot_grads.at[target].set(
        pair_grad.reshape(tiles_here * tile_cap, sample_count * coeff_dim), mode="drop"
    )
    slot_like = jnp.zeros((slot_count, sample_count), jnp.float32)
    slot_like = slot_like.at[target].set(
        pair_like.reshape(tiles_here * tile_cap, sample_count), mode="drop"
    )
    back_grads, back_like = (
        lax.all_to_all(
            slot_grads.reshape(sky_count, send_cap, sample_count * coeff_dim),
            "sky",
            split_axis=0,
            concat_axis=0,
            tiled=True,
        ),
        lax.all_to_all(
            slot_like.reshape(sky_count, send_cap, sample_count),
            "sky",
            split_axis=0,
            concat_axis=0,
            tiled=True,
        ),
    )
    grad_part = galaxy_sums(sent_rows, back_grads, galaxy_count).reshape(
        galaxy_count, sample_count, coeff_dim
    )
    like_part = galaxy_sums(sent_rows, back_like, galaxy_count)
    like_out, grad_out = (
        lax.psum_scatter(like_part, "expo", scatter_dimension=1, tiled=True),
        lax.psum_scatter(grad_part, "expo", scatter_dimension=1, tiled=True),
    )
    return (like_out, grad_out)


def solution(mesh):
    placed = (
        P("sky", None, None),
        P(),
        P(("expo", "sky"), None, None),
        P(("expo", "sky"), None, None),
        P(("expo", "sky"), None, None),
        P("expo", "sky", None, None),
        P(("expo", "sky"), None),
    )
    return jax.shard_map(
        per_device,
        mesh=mesh,
        in_specs=placed,
        out_specs=(P("sky", "expo"), P("sky", "expo", None)),
        check_vma=False,
    )
```

profile of v0, /device:TPU:1, one launch (start us, length us, event | category | flops | bytes accessed | tf_op | source)
XLA Modules:
  0.0 384.2 jit_solution(5767647732668749701)
XLA Ops:
  7.2 0.0 copy-start
  7.2 0.8 broadcast_maximum_fusion
  7.9 0.7 broadcast_compare_fusion
  8.6 1.9 copy.23
  10.5 0.1 copy.18
  10.6 0.1 reshape.124
  10.7 4.2 %gather_fusion = bf16[192,8192]{1,0:T(8,128)(2,1)} fusion(bf16[64,8192]{1,0:T(8,128)(2,1)S(1)} %bitcast.44, s32[1024]{0:T(1024)S(1)} %pad_clamp_fusion.1), kind=kCustom, calls=%fused_computation | custom fusion | bytes 6292224 | tf_op jit(solution)/shard_map/jit(_take)/gather | solution.py:24
  14.9 4.7 %reshape.123 = bf16[16,12,8192]{2,1,0:T(8,128)(2,1)} reshape(bf16[192,8192]{1,0:T(8,128)(2,1)} %gather_fusion) | data formatting | bytes 6291456 | tf_op jit(solution)/shard_map/jit(_take)/gather | solution.py:24
  19.6 0.1 copy.21
  19.7 4.6 %broadcast_select_fusion = bf16[16,12,8192]{2,1,0:T(8,128)(2,1)} fusion(bf16[16,12,8192]{2,1,0:T(8,128)(2,1)} %reshape.123, pred[16,12]{1,0:T(8,128)(4,1)S(1)} %bitcast.49), kind=kLoop, calls=%fused_computation.15 | loop fusion | flops 1572864 | bytes 6291648 | tf_op jit(solution)/shard_map/jit(_take)/select_n | solution.py:24
  24.3 0.0 copy-start.3
  24.3 7.8 %all-to-all-start = ((bf16[16,12,8192]{2,1,0:T(8,128)(2,1)}), bf16[16,12,8192]{2,1,0:T(8,128)(2,1)}, u32[]{:S(2)}, u32[]{:S(2)}) async-start(bf16[16,12,8192]{2,1,0:T(8,128)(2,1)} %broadcast_select_fusion), calls=%async_computation | async-start | bytes 8388608 | tf_op jit(solution)/shard_map/all_to_all | solution.py:25
  32.1 0.0 copy-done.3
  32.1 0.1 reshape.112
  32.2 0.1 reshape.132
  32.3 60.1 %all-to-all-done = bf16[16,12,8192]{2,1,0:T(8,128)(2,1)} async-done(((bf16[16,12,8192]{2,1,0:T(8,128)(2,1)}), bf16[16,12,8192]{2,1,0:T(8,128)(2,1)}, u32[]{:S(2)}, u32[]{:S(2)}) %all-to-all-start) | async-done | bytes 3145760 | tf_op jit(solution)/shard_map/all_to_all | solution.py:25
  92.4 4.7 %reshape.114 = bf16[192,8192]{1,0:T(8,128)(2,1)} reshape(bf16[16,12,8192]{2,1,0:T(8,128)(2,1)} %all-to-all-done) | data formatting | bytes 6291456 | tf_op jit(solution)/shard_map/reshape | solution.py:26
  97.1 6.1 %gather_fusion.1 = bf16[128,8192]{1,0:T(8,128)(2,1)S(1)} fusion(bf16[192,8192]{1,0:T(8,128)(2,1)} %reshape.114, s32[1024]{0:T(1024)S(1)} %pad_clamp_fusion), kind=kCustom, calls=%fused_computation.1 | custom fusion | bytes 4194816 | tf_op jit(solution)/shard_map/jit(_take)/gather | solution.py:28
  103.1 1.6 broadcast_select_fusion.1
  104.8 2.9 select_n.37
  107.6 0.0 copy-done
  107.6 0.0 copy-start.1
  107.7 5.6 %convolution_convert_fusion = bf16[4096,1024]{1,0:T(8,128)(2,1)} fusion(bf16[4096,256]{1,0:T(8,128)(2,1)S(1)} %select_n.37, bf16[256,1024]{1,0:T(8,128)(2,1)S(1)} %copy-done), kind=kOutput, calls=%fused_computation.9 | convolution fusion | flops 2151677952 | bytes 11010048 | tf_op jit(solution)/shard_map/dot_general | solution.py:29
  113.2 0.0 copy-done.1
  113.2 19.0 %fusion = (bf16[8,512,1024]{2,1,0:T(8,128)(2,1)}, f32[8,512]{1,0:T(8,128)S(1)}) fusion(f32[8,16,1024]{2,1,0:T(8,128)S(1)} %copy-done.1, f32[8,16,1024]{2,1,0:T(8,128)} %param.11, bf16[8,512,1024]{2,1,0:T(8,128)(2,1)} %bitcast.45, bf16[8,1024,1024]{2,1,0:T(8,128)(2,1)} %param.9), kind=kOutput, calls=%fused_computation.6 | convolution fusion | flops 8610902016 | bytes 34619392 | tf_op jit(solution)/shard_map/tnp,tpq->tnq/dot_general | solution.py:31
  132.2 15.7 %convolution_convert_fusion.1 = bf16[8,512,1024]{2,1,0:T(8,128)(2,1)} fusion(bf16[8,512,1024]{2,1,0:T(8,128)(2,1)} %get-tuple-element.8, bf16[8,1024,1024]{2,1,0:T(8,128)(2,1)} %param.9), kind=kOutput, calls=%fused_computation.10 | convolution fusion | flops 8594128896 | bytes 33554432 | tf_op jit(solution)/shard_map/tnq,tpq->tnp/dot_general | solution.py:37
  147.9 7.7 %convolution_multiply_fusion = f32[4096,256]{1,0:T(8,128)} fusion(bf16[4096,1024]{1,0:T(8,128)(2,1)} %bitcast.50, bf16[256,1024]{1,0:T(8,128)(2,1)S(1)} %copy-done), kind=kOutput, calls=%fused_computation.14 | convolution fusion | flops 2148532224 | bytes 13107200 | tf_op jit(solution)/shard_map/dot_general | solution.py:43
  155.6 5.0 %reshape.150 = f32[128,8192]{1,0:T(8,128)} reshape(f32[4096,256]{1,0:T(8,128)} %convolution_multiply_fusion) | data formatting | bytes 8388608 | tf_op jit(solution)/shard_map/reshape | solution.py:53
  160.7 7.5 %scatter_custom_fusion.1 = f32[192,8192]{1,0:T(8,128)} fusion(s32[128]{0:T(128)S(1)} %fusion.15, f32[128,8192]{1,0:T(8,128)} %reshape.150, f32[]{:T(128)} %constant.22.clone.1), kind=kCustom, calls=%fused_computation.16 | custom fusion | bytes 6291968 | tf_op jit(solution)/shard_map/scatter | solution.py:52
  168.1 6.5 %reshape.120 = f32[16,12,8192]{2,1,0:T(8,128)} reshape(f32[192,8192]{1,0:T(8,128)} %scatter_custom_fusion.1) | data formatting | bytes 12582912 | tf_op jit(solution)/shard_map/reshape | solution.py:61
  174.7 0.0 copy-start.2
  174.7 11.6 %all-to-all-start.2 = ((f32[16,12,8192]{2,1,0:T(8,128)}), f32[16,12,8192]{2,1,0:T(8,128)}, u32[]{:S(2)}, u32[]{:S(2)}) async-start(f32[16,12,8192]{2,1,0:T(8,128)} %reshape.120), calls=%async_computation.2 | async-start | bytes 16777216 | tf_op jit(solution)/shard_map/all_to_all | solution.py:60
  186.2 0.0 reduce-scatter.2.cloned.1.call-start
  186.3 0.0 copy-done.2
  186.3 0.1 copy.16
  186.4 0.1 eq.8
  186.5 129.0 %all-to-all-done.2 = f32[16,12,8192]{2,1,0:T(8,128)} async-done(((f32[16,12,8192]{2,1,0:T(8,128)}), f32[16,12,8192]{2,1,0:T(8,128)}, u32[]{:S(2)}, u32[]{:S(2)}) %all-to-all-start.2) | async-done | bytes 6291488 | tf_op jit(solution)/shard_map/all_to_all | solution.py:60
  315.5 6.5 %reshape.121 = f32[192,8192]{1,0:T(8,128)} reshape(f32[16,12,8192]{2,1,0:T(8,128)} %all-to-all-done.2) | data formatting | bytes 12582912 | tf_op jit(solution)/shard_map/reshape | solution.py:12
  322.0 0.0 copy-start.4
  322.0 6.8 %fusion.3 = f32[64,32,256]{2,0,1:T(8,128)} fusion(f32[24,32,8,256]{3,2,1,0:T(8,128)} %bitcast.46, s32[192]{0:T(256)S(1)} %eq.8), kind=kOutput, calls=%fused_computation.11 | convolution fusion | flops 1207971840 | bytes 8389376 | tf_op jit(solution)/shard_map/dot_general | solution.py:12
  328.8 0.0 reduce-scatter.2.cloned.1.call-update
  328.9 0.1 reshape.142
  328.9 0.9 scatter_custom_fusion
  329.9 0.7 reshape.164
  330.6 10.1 %all-to-all-start.1 = ((f32[16,1,384]{2,1,0:T(1,128)}), f32[16,1,384]{2,1,0:T(1,128)S(1)}, u32[]{:S(2)}, u32[]{:S(2)}) async-start(f32[16,1,384]{2,1,0:T(1,128)} %reshape.164), calls=%async_computation.1 | async-start | bytes 49152 | tf_op jit(solution)/shard_map/all_to_all | solution.py:67
  340.7 0.0 copy-done.4
  340.7 0.6 dynamic-slice
  342.0 5.2 %all-to-all-done.1 = f32[16,1,384]{2,1,0:T(1,128)S(1)} async-done(((f32[16,1,384]{2,1,0:T(1,128)}), f32[16,1,384]{2,1,0:T(1,128)S(1)}, u32[]{:S(2)}, u32[]{:S(2)}) %all-to-all-start.1) | async-done | bytes 24608 | tf_op jit(solution)/shard_map/all_to_all | solution.py:67
  347.2 0.5 broadcast.81
  347.7 0.7 reduce.1
  348.4 0.1 reshape.165
  348.5 0.2 fusion.9
  348.7 26.2 %all-reduce = f32[64,32]{0,1:T(8,128)S(1)} all-reduce(f32[64,32]{0,1:T(8,128)S(1)} %fusion.9), channel_id=2, replica_groups=mesh['expo'=8,'sky'=16] {'expo'}, use_global_device_ids=true, to_apply=%region_2.3.clone | all-reduce | flops 2048 | bytes 16384
  375.0 0.6 constant_dynamic-slice_fusion
  375.6 0.0 reduce-scatter.2.cloned.1.call-done
  375.6 1.8 copy.20
  (8 shorter events, 0.1 us)
Async XLA Ops:
  7.2 100.5 %copy-start = (bf16[256,1024]{1,0:T(8,128)(2,1)S(1)}, bf16[256,1024]{1,0:T(8,128)(2,1)}, u32[]{:S(2)}) copy-start(bf16[256,1024]{1,0:T(8,128)(2,1)} %param.8) | copy-start | bytes 1572868
  24.3 7.8 %copy-start.3 = (s32[8,16]{1,0:T(8,128)S(1)}, s32[8,16]{1,0:T(8,128)}, u32[]{:S(2)}) copy-start(s32[8,16]{1,0:T(8,128)} %param.13) | copy-start | bytes 1540
  24.3 68.1 %all-to-all-start = ((bf16[16,12,8192]{2,1,0:T(8,128)(2,1)}), bf16[16,12,8192]{2,1,0:T(8,128)(2,1)}, u32[]{:S(2)}, u32[]{:S(2)}) async-start(bf16[16,12,8192]{2,1,0:T(8,128)(2,1)} %broadcast_select_fusion), calls=%async_computation | async-start | bytes 8388608 | tf_op jit(solution)/shard_map/all_to_all | solution.py:25
  107.6 5.6 %copy-start.1 = (f32[8,16,1024]{2,1,0:T(8,128)S(1)}, f32[8,16,1024]{2,1,0:T(8,128)}, u32[]{:S(2)}) copy-start(f32[8,16,1024]{2,1,0:T(8,128)} %param.10) | copy-start | bytes 1572868
  174.7 11.6 %copy-start.2 = (s32[1,1,16,12]{2,1,3,0:T(1,128)S(1)}, s32[1,1,16,12]{2,1,3,0:T(1,128)}, u32[]{:S(2)}) copy-start(s32[1,1,16,12]{2,1,3,0:T(1,128)} %param.12) | copy-start | bytes 2308
  174.7 140.8 %all-to-all-start.2 = ((f32[16,12,8192]{2,1,0:T(8,128)}), f32[16,12,8192]{2,1,0:T(8,128)}, u32[]{:S(2)}, u32[]{:S(2)}) async-start(f32[16,12,8192]{2,1,0:T(8,128)} %reshape.120), calls=%async_computation.2 | async-start | bytes 16777216 | tf_op jit(solution)/shard_map/all_to_all | solution.py:60
  186.2 189.3 %reduce-scatter.2.cloned.1.call-start = ((), (), s32[]{:S(2)}) async-start(), calls=%async_computation.4 | async-start | bytes 2359296 | tf_op jit(solution)/shard_map/reduce_scatter | solution.py:81
  322.0 18.7 %copy-start.4 = (u32[128]{0:T(128)S(1)}, u32[128]{0:T(128)}, u32[]{:S(2)}) copy-start(u32[128]{0:T(128)} %constant.53) | copy-start | bytes 1540
  330.6 16.6 %all-to-all-start.1 = ((f32[16,1,384]{2,1,0:T(1,128)}), f32[16,1,384]{2,1,0:T(1,128)S(1)}, u32[]{:S(2)}, u32[]{:S(2)}) async-start(f32[16,1,384]{2,1,0:T(1,128)} %reshape.164), calls=%async_computation.1 | async-start | bytes 49152 | tf_op jit(solution)/shard_map/all_to_all | solution.py:67
Sparse Core Ops, SparseCore 0:
  329.0 40.4 reduce-scatter.1
where the time goes:
time: 387 us; the launch traced here: 384 us
  waiting for transfers between devices  194 us (50%)
  local copies, waits for them, and re-layouts  55.8 us (14%)
  matrix products  55 us (14%)
  starting transfers between devices  29.5 us (8%)
  blocking collectives  26.2 us (7%)
  between operations  14.9 us (4%)
  other arithmetic  8.43 us (2%)
    all_to_all x1, waiting for transfers between devices, per_device(): lax.all_to_all(slot_grads.reshape(sky_count, send_cap, sample_count * coe...  129 us
    all_to_all x1, waiting for transfers between devices, per_device(): lax.all_to_all(outgoing, 'sky', split_axis=0, concat_axis=0, tiled=True)  60.1 us
    unnamed x1, blocking collectives  26.2 us
    dot_general x1, matrix products, per_device(): jnp.einsum('tnp,tpq->tnq', rendered, operators, preferred_element_type=jn...  19 us
    dot_general x1, matrix products, per_device(): jnp.einsum('tnq,tpq->tnp', scaled, operators, preferred_element_type=jnp....  15.7 us
    all_to_all x1, starting transfers between devices, per_device(): lax.all_to_all(slot_grads.reshape(sky_count, send_cap, sample_count * coe...  11.6 us
    all_to_all x1, starting transfers between devices, per_device(): lax.all_to_all(slot_like.reshape(sky_count, send_cap, sample_count), 'sky...  10.1 us
    gather x2, local copies, waits for them, and re-layouts, per_device(): outgoing = jnp.take(flat_samples, jnp.maximum(sent_rows, 0), axis=0)  8.88 us
  transfers between devices with their start and end apart: 4, of which 3 were waited for; matrix products, arithmetic and copies ran while one was open for 1% of the time, Pallas kernels for 0%

commit v1 on v0

v1 whole, which is shorter than its diff:
```python
import jax
import jax.numpy as jnp
from jax import lax
from jax.sharding import PartitionSpec as P

N_CHUNKS = 2
LANE = 128


def galaxy_sums(listed, values, galaxy_count):
    flat_list = listed.reshape(-1)
    onehot = (flat_list[None, :] == jnp.arange(galaxy_count, dtype=jnp.int32)[:, None]).astype(
        jnp.float32
    )
    return jnp.dot(onehot, values.reshape(flat_list.shape[0], -1), precision=lax.Precision.HIGHEST)


def per_device(samples, basis, operators, cutouts, pixel_weights, detections, intersections):
    tiles_here, tile_cap, pixels = cutouts.shape
    coeff_dim = basis.shape[0]
    galaxy_count, sample_count, _unused = samples.shape
    sky_count = lax.axis_size("sky")
    expo_count = lax.axis_size("expo")
    send_cap = detections.shape[3]
    slot_count = sky_count * send_cap
    per_expo = sample_count // expo_count
    chunk_size = per_expo // N_CHUNKS
    chunk_samples = expo_count * chunk_size
    sent_rows = detections.reshape(sky_count, send_cap)
    positions = tiles_here * tile_cap

    outgoing = jnp.take(samples, jnp.maximum(sent_rows, 0), axis=0)
    outgoing = outgoing.reshape(sky_count, send_cap, expo_count, N_CHUNKS, chunk_size, coeff_dim)
    live = intersections >= 0
    pick = jnp.maximum(intersections, 0).reshape(-1)
    target = jnp.where(live, intersections, slot_count).reshape(-1)
    grad_width = chunk_samples * coeff_dim
    width = grad_width + LANE

    grad_pieces = []
    like_pieces = []
    for chunk in range(N_CHUNKS):
        sent = outgoing[:, :, :, chunk].reshape(sky_count, send_cap, chunk_samples * coeff_dim)
        incoming = lax.all_to_all(sent, "sky", split_axis=0, concat_axis=0, tiled=True)
        incoming = incoming.reshape(slot_count, chunk_samples * coeff_dim)
        picked = jnp.take(incoming, pick, axis=0).reshape(-1, coeff_dim)
        rendered = jnp.dot(picked, basis, preferred_element_type=jnp.float32).astype(jnp.bfloat16)
        rendered = rendered.reshape(tiles_here, tile_cap * chunk_samples, pixels)
        model = jnp.einsum("tnp,tpq->tnq", rendered, operators, preferred_element_type=jnp.float32)
        model = model.reshape(tiles_here, tile_cap, chunk_samples, pixels)
        resid = model - cutouts[:, :, None, :]
        weighted = pixel_weights[:, :, None, :] * resid
        pair_like = -0.5 / pixels * jnp.sum(weighted * resid, axis=-1)
        scaled = weighted.astype(jnp.bfloat16).reshape(tiles_here, tile_cap * chunk_samples, pixels)
        backed = jnp.einsum(
            "tnq,tpq->tnp", scaled, operators, preferred_element_type=jnp.float32
        ).astype(jnp.bfloat16)
        pair_grad = (
            -1.0
            / pixels
            * lax.dot_general(
                backed.reshape(-1, pixels),
                basis,
                (((1,), (1,)), ((), ())),
                preferred_element_type=jnp.float32,
            )
        )
        payload = jnp.concatenate(
            [
                pair_grad.reshape(positions, grad_width),
                pair_like.reshape(positions, chunk_samples),
                jnp.zeros((positions, LANE - chunk_samples), jnp.float32),
            ],
            axis=1,
        )
        slot_payload = jnp.zeros((slot_count, width), jnp.float32)
        slot_payload = slot_payload.at[target].set(payload, mode="drop")
        back = lax.all_to_all(
            slot_payload.reshape(sky_count, send_cap, width),
            "sky",
            split_axis=0,
            concat_axis=0,
            tiled=True,
        )
        summed = galaxy_sums(sent_rows, back, galaxy_count)
        grads = summed[:, :grad_width].reshape(galaxy_count, expo_count, chunk_size * coeff_dim)
        likes = summed[:, grad_width : grad_width + chunk_samples].reshape(
            galaxy_count, expo_count, chunk_size
        )
        like_rows = likes.transpose(1, 2, 0).reshape(1, chunk_samples, galaxy_count)
        flat = jnp.concatenate(
            [
                grads.reshape(galaxy_count, chunk_samples, coeff_dim),
                jnp.pad(like_rows, ((0, 0), (0, 0), (0, coeff_dim - galaxy_count))),
            ],
            axis=0,
        )
        mine = lax.psum_scatter(flat, "expo", scatter_dimension=1, tiled=True)
        grad_pieces.append(mine[:galaxy_count])
        like_pieces.append(mine[galaxy_count, :, :galaxy_count].T)
    grad_out = jnp.concatenate(grad_pieces, axis=1)
    like_out = jnp.concatenate(like_pieces, axis=1)
    return (like_out, grad_out)


def solution(mesh):
    placed = (
        P("sky", None, None),
        P(),
        P(("expo", "sky"), None, None),
        P(("expo", "sky"), None, None),
        P(("expo", "sky"), None, None),
        P("expo", "sky", None, None),
        P(("expo", "sky"), None),
    )
    return jax.shard_map(
        per_device,
        mesh=mesh,
        in_specs=placed,
        out_specs=(P("sky", "expo"), P("sky", "expo", None)),
        check_vma=False,
    )
```

time: 387 us -> 340 us (0.88)
  waiting for transfers between devices: 194 us -> 138 us
  blocking collectives: 26.2 us -> 0 us
  local copies, waits for them, and re-layouts: 55.8 us -> 74.4 us
  matrix products: 55 us -> 70.4 us
    all_to_all x3 -> x4, waiting for transfers between devices: 194 us -> 100 us  [the longest x2 58.2 us: per_device(): lax.all_to_all(slot_payload.reshape(sky_count, send_cap, width), 'sky', s...]
    reduce_scatter x1 -> x2, waiting for transfers between devices: 0.01 us -> 37.8 us  [per_device(): mine = lax.psum_scatter(flat, 'expo', scatter_dimension=1, tiled=True)]
    unnamed x1 -> x0, blocking collectives: 26.2 us -> none
    another operation x0 -> x7, local copies, waits for them, and re-layouts: none -> 12.9 us  [the longest x4 12.6 us: per_device(): outgoing[:, :, :, chunk]]
    dot_general x1 -> x2, matrix products: 19 us -> 26.9 us  [per_device(): jnp.einsum('tnp,tpq->tnq', rendered, operators, preferred_element_type=jn...]
    slice x0 -> x11, local copies, waits for them, and re-layouts: none -> 7.02 us  [the longest x1 3.52 us: per_device(): outgoing[:, :, :, chunk]]
    dot_general x1 -> x2, matrix products: 15.7 us -> 21.6 us  [per_device(): jnp.einsum('tnq,tpq->tnp', scaled, operators, preferred_element_type=jnp....]
    unnamed x17 -> x21, local copies, waits for them, and re-layouts: 5.75 us -> 1.01 us
  transfers between devices with their start and end apart: 4 -> 6, of which waited for: 3 -> 5; matrix products, arithmetic and copies ran while one was open for 1% -> 18% of each run, Pallas kernels for 0% -> 0%
where the time goes in v1:
time: 340 us; the launch traced here: 336 us
  waiting for transfers between devices  138 us (41%)
  local copies, waits for them, and re-layouts  74.4 us (22%)
  matrix products  70.4 us (21%)
  starting transfers between devices  27.9 us (8%)
  between operations  14.4 us (4%)
  other arithmetic  10.8 us (3%)
    all_to_all x2, waiting for transfers between devices, per_device(): lax.all_to_all(slot_payload.reshape(sky_count, send_cap, width), 'sky', s...  58.2 us
    all_to_all x2, waiting for transfers between devices, per_device(): lax.all_to_all(sent, 'sky', split_axis=0, concat_axis=0, tiled=True)  42 us
    reduce_scatter x2, waiting for transfers between devices, per_device(): mine = lax.psum_scatter(flat, 'expo', scatter_dimension=1, tiled=True)  37.8 us
    dot_general x2, matrix products, per_device(): jnp.einsum('tnp,tpq->tnq', rendered, operators, preferred_element_type=jn...  26.9 us
    dot_general x2, matrix products, per_device(): jnp.einsum('tnq,tpq->tnp', scaled, operators, preferred_element_type=jnp....  21.6 us
    all_to_all x2, starting transfers between devices, per_device(): lax.all_to_all(slot_payload.reshape(sky_count, send_cap, width), 'sky', s...  15.6 us
    another operation x4, local copies, waits for them, and re-layouts, per_device(): outgoing[:, :, :, chunk]  12.6 us
    all_to_all x2, starting transfers between devices, per_device(): lax.all_to_all(sent, 'sky', split_axis=0, concat_axis=0, tiled=True)  12.2 us
  transfers between devices with their start and end apart: 6, of which 5 were waited for; matrix products, arithmetic and copies ran while one was open for 18% of the time, Pallas kernels for 0%

profile of v1, /device:TPU:1, one launch (start us, length us, event | category | flops | bytes accessed | tf_op | source)
XLA Modules:
  0.0 336.0 jit_solution(2700478431737591492)
XLA Ops:
  7.2 0.8 broadcast_compare_fusion
  8.0 0.7 broadcast_maximum_fusion
  8.7 0.1 copy.20
  8.8 0.1 reshape.187
  8.9 2.6 gather_fusion
  11.5 5.7 %gather.10 = bf16[16,12,8,2,2,256]{5,4,3,2,1,0:T(2,128)(2,1)} reshape(bf16[192,32,256]{2,1,0:T(8,128)(2,1)} %gather_fusion) | data formatting | bytes 6291456 | tf_op jit(solution)/shard_map/jit(_take)/gather | solution.py:32
  17.2 4.9 %broadcast_select_fusion = bf16[16,12,8,2,2,256]{5,4,2,0,1,3:T(2,128)(2,1)S(1)} fusion(pred[16,12]{0,1:T(8,128)(4,1)S(1)} %bitcast.97, bf16[16,12,8,2,2,256]{5,4,3,2,1,0:T(2,128)(2,1)} %gather.10), kind=kLoop, calls=%fused_computation.15 | loop fusion | flops 1572864 | bytes 6291648 | tf_op jit(solution)/shard_map/jit(_take)/select_n | solution.py:32
  22.2 3.5 %fusion.15 = (bf16[16,12,8,1,2,256]{5,4,2,0,1,3:T(2,128)(2,1)}, bf16[16,12,8,1,2,256]{5,4,2,0,1,3:T(2,128)(2,1)}) fusion(bf16[16,12,8,2,2,256]{5,4,2,0,1,3:T(2,128)(2,1)S(1)} %broadcast_select_fusion), kind=kLoop, calls=%fused_computation.53 | loop fusion | bytes 6291456 | tf_op jit(solution)/shard_map/slice | solution.py:43
  25.7 2.9 reshape_squeeze.6
  28.5 2.2 copy.22
  30.8 7.6 %all-to-all-start = ((bf16[16,12,4096]{2,1,0:T(8,128)(2,1)}), bf16[16,12,4096]{2,1,0:T(8,128)(2,1)S(1)}, u32[]{:S(2)}, u32[]{:S(2)}) async-start(bf16[16,12,4096]{2,1,0:T(8,128)(2,1)} %copy.22), calls=%async_computation | async-start | bytes 4194304 | tf_op jit(solution)/shard_map/all_to_all | solution.py:44
  38.3 3.9 %reshape_squeeze.7 = bf16[16,12,4096]{2,0,1:T(8,128)(2,1)} reshape(bf16[16,12,8,1,2,256]{5,4,2,0,1,3:T(2,128)(2,1)} %get-tuple-element.10) | data formatting | bytes 3145728 | tf_op jit(solution)/shard_map/reshape;squeeze | solution.py:43
  42.2 3.7 %copy.26 = bf16[16,12,4096]{2,1,0:T(8,128)(2,1)} copy(bf16[16,12,4096]{2,0,1:T(8,128)(2,1)} %reshape_squeeze.7) | data formatting | bytes 3145728 | tf_op jit(solution)/shard_map/reshape;squeeze | solution.py:43
  45.9 20.6 %all-to-all-done = bf16[16,12,4096]{2,1,0:T(8,128)(2,1)S(1)} async-done(((bf16[16,12,4096]{2,1,0:T(8,128)(2,1)}), bf16[16,12,4096]{2,1,0:T(8,128)(2,1)S(1)}, u32[]{:S(2)}, u32[]{:S(2)}) %all-to-all-start) | async-done | bytes 1572896 | tf_op jit(solution)/shard_map/all_to_all | solution.py:44
  66.5 4.6 %all-to-all-start.2 = ((bf16[16,12,4096]{2,1,0:T(8,128)(2,1)}), bf16[16,12,4096]{2,1,0:T(8,128)(2,1)}, u32[]{:S(2)}, u32[]{:S(2)}) async-start(bf16[16,12,4096]{2,1,0:T(8,128)(2,1)} %copy.26), calls=%async_computation.3 | async-start | bytes 4194304 | tf_op jit(solution)/shard_map/all_to_all | solution.py:44
  71.2 0.1 reshape.149
  71.2 0.1 reshape.151
  71.4 2.5 reshape.150
  73.8 1.2 gather_fusion.1
  75.0 21.4 %all-to-all-done.2 = bf16[16,12,4096]{2,1,0:T(8,128)(2,1)} async-done(((bf16[16,12,4096]{2,1,0:T(8,128)(2,1)}), bf16[16,12,4096]{2,1,0:T(8,128)(2,1)}, u32[]{:S(2)}, u32[]{:S(2)}) %all-to-all-start.2) | async-done | bytes 1572896 | tf_op jit(solution)/shard_map/all_to_all | solution.py:44
  96.4 2.5 reshape.160
  98.9 2.2 gather_fusion.2
  101.1 1.5 broadcast_select_fusion.2
  102.6 0.5 reshape.161
  103.1 0.5 reshape.152
  103.6 2.4 convolution_convert_fusion
  106.0 3.2 convolution_convert_fusion.1
  109.2 12.7 %fusion.16 = f32[8,256,1024]{2,1,0:T(8,128)} fusion(bf16[8,256,1024]{2,1,0:T(8,128)(2,1)S(1)} %bitcast.90, bf16[8,1024,1024]{2,1,0:T(8,128)(2,1)} %param.11), kind=kOutput, calls=%fused_computation.54 | convolution fusion | flops 4294967296 | bytes 29360128 | tf_op jit(solution)/shard_map/tnp,tpq->tnq/dot_general | solution.py:49
  121.9 14.2 %fusion.5 = (f32[8,256]{1,0:T(8,128)S(1)}, f32[8,256]{1,0:T(8,128)S(1)}, bf16[8,256,1024]{2,1,0:T(8,128)(2,1)}, bf16[8,256,1024]{2,1,0:T(8,128)(2,1)}) fusion(f32[8,16,1024]{2,1,0:T(8,128)S(1)} %copy-done.5, f32[8,16,1024]{2,1,0:T(8,128)S(1)} %copy-done.6, f32[8,256,1024]{2,1,0:T(8,128)} %fusion.16, bf16[8,256,1024]{2,1,0:T(8,128)(2,1)} %bitcast.89, ...), kind=kOutput, calls=%fused_computation.14 | convolution fusion | flops 4315934720 | bytes 38813696 | tf_op jit(solution)/shard_map/tnp,tpq->tnq/dot_general | solution.py:49
  136.1 10.8 %convolution_convert_fusion.2 = bf16[8,256,1024]{2,1,0:T(8,128)(2,1)} fusion(bf16[8,256,1024]{2,1,0:T(8,128)(2,1)} %get-tuple-element.8, bf16[8,1024,1024]{2,1,0:T(8,128)(2,1)} %param.11), kind=kOutput, calls=%fused_computation.20 | convolution fusion | flops 4297064448 | bytes 25165824 | tf_op jit(solution)/shard_map/tnq,tpq->tnp/dot_general | solution.py:55
  146.9 4.8 %convolution_multiply_fusion = f32[2048,256]{1,0:T(8,128)} fusion(bf16[2048,1024]{1,0:T(8,128)(2,1)} %bitcast.100, bf16[256,1024]{1,0:T(8,128)(2,1)S(1)} %copy-done.3), kind=kOutput, calls=%fused_computation.18 | convolution fusion | flops 1074266112 | bytes 6815744 | tf_op jit(solution)/shard_map/dot_general | solution.py:61
  151.7 1.7 reshape.164
  153.5 0.1 mul.59
  153.6 2.1 concatenate.20
  155.7 4.7 %scatter_custom_fusion.1 = f32[192,4224]{1,0:T(8,128)} fusion(s32[128]{0:T(128)S(1)} %fusion.14, f32[128,4224]{1,0:T(8,128)} %concatenate.20, f32[]{:T(128)} %constant.15.clone.1), kind=kCustom, calls=%fused_computation.22 | custom fusion | bytes 3244544 | tf_op jit(solution)/shard_map/scatter | solution.py:77
  160.5 4.3 %reshape.165 = f32[16,12,4224]{2,1,0:T(8,128)} reshape(f32[192,4224]{1,0:T(8,128)} %scatter_custom_fusion.1) | data formatting | bytes 6488064 | tf_op jit(solution)/shard_map/reshape | solution.py:79
  164.8 6.6 %all-to-all-start.3 = ((f32[16,12,4224]{2,1,0:T(8,128)}), f32[16,12,4224]{2,1,0:T(8,128)}, u32[]{:S(2)}, u32[]{:S(2)}) async-start(f32[16,12,4224]{2,1,0:T(8,128)} %reshape.165), calls=%async_computation.4 | async-start | bytes 8650752 | tf_op jit(solution)/shard_map/all_to_all | solution.py:78
  171.4 10.8 %convolution_convert_fusion.3 = bf16[8,256,1024]{2,1,0:T(8,128)(2,1)} fusion(bf16[8,256,1024]{2,1,0:T(8,128)(2,1)} %get-tuple-element.7, bf16[8,1024,1024]{2,1,0:T(8,128)(2,1)} %param.11), kind=kOutput, calls=%fused_computation.21 | convolution fusion | flops 4297064448 | bytes 25165824 | tf_op jit(solution)/shard_map/tnq,tpq->tnp/dot_general | solution.py:55
  182.2 4.8 %convolution_multiply_fusion.1 = f32[2048,256]{1,0:T(8,128)} fusion(bf16[2048,1024]{1,0:T(8,128)(2,1)} %bitcast.101, bf16[256,1024]{1,0:T(8,128)(2,1)S(1)} %copy-done.4), kind=kOutput, calls=%fused_computation.19 | convolution fusion | flops 1074266112 | bytes 6815744 | tf_op jit(solution)/shard_map/dot_general | solution.py:61
  187.1 1.7 reshape.155
  188.8 0.1 mul.54
  188.9 2.2 concatenate.18
  191.1 4.7 %scatter_custom_fusion = f32[192,4224]{1,0:T(8,128)} fusion(s32[128]{0:T(128)S(1)} %fusion.14, f32[128,4224]{1,0:T(8,128)} %concatenate.18, f32[]{:T(128)} %constant.15.clone.1), kind=kCustom, calls=%fused_computation.24 | custom fusion | bytes 3244544 | tf_op jit(solution)/shard_map/scatter | solution.py:77
  195.8 4.3 %reshape.156 = f32[16,12,4224]{2,1,0:T(8,128)} reshape(f32[192,4224]{1,0:T(8,128)} %scatter_custom_fusion) | data formatting | bytes 6488064 | tf_op jit(solution)/shard_map/reshape | solution.py:79
  200.1 20.1 %all-to-all-done.3 = f32[16,12,4224]{2,1,0:T(8,128)} async-done(((f32[16,12,4224]{2,1,0:T(8,128)}), f32[16,12,4224]{2,1,0:T(8,128)}, u32[]{:S(2)}, u32[]{:S(2)}) %all-to-all-start.3) | async-done | bytes 3244064 | tf_op jit(solution)/shard_map/all_to_all | solution.py:78
  220.2 9.0 %all-to-all-start.1 = ((f32[16,12,4224]{2,1,0:T(8,128)}), f32[16,12,4224]{2,1,0:T(8,128)}, u32[]{:S(2)}, u32[]{:S(2)}) async-start(f32[16,12,4224]{2,1,0:T(8,128)} %reshape.156), calls=%async_computation.1 | async-start | bytes 8650752 | tf_op jit(solution)/shard_map/all_to_all | solution.py:78
  229.3 0.1 copy.19
  229.4 0.1 eq.8
  229.5 4.7 %reshape.166 = f32[192,4224]{1,0:T(8,128)} reshape(f32[16,12,4224]{2,1,0:T(8,128)} %all-to-all-done.3) | data formatting | bytes 6488064 | tf_op jit(solution)/shard_map/reshape | solution.py:15
  234.2 3.4 fusion.10
  237.7 0.1 copy.38
  237.8 1.2 select_maximum_fusion
  239.0 38.1 %all-to-all-done.1 = f32[16,12,4224]{2,1,0:T(8,128)} async-done(((f32[16,12,4224]{2,1,0:T(8,128)}), f32[16,12,4224]{2,1,0:T(8,128)}, u32[]{:S(2)}, u32[]{:S(2)}) %all-to-all-start.1) | async-done | bytes 3244064 | tf_op jit(solution)/shard_map/all_to_all | solution.py:78
  277.1 4.7 %reshape.157 = f32[192,4224]{1,0:T(8,128)} reshape(f32[16,12,4224]{2,1,0:T(8,128)} %all-to-all-done.1) | data formatting | bytes 6488064 | tf_op jit(solution)/shard_map/reshape | solution.py:15
  281.8 3.4 fusion.11
  285.3 0.1 copy.39
  285.4 1.1 select_maximum_fusion.1
  286.6 0.9 slice.55
  287.5 37.8 %reduce-scatter.3.cloned.1.call-done = f32[65,2,256]{2,0,1:T(8,128)} async-done(((f32[65,16,256]{2,0,1:T(8,128)}), f32[65,2,256]{2,0,1:T(8,128)}) %reduce-scatter.3.cloned.1.call-update) | async-done | bytes 133136 | tf_op jit(solution)/shard_map/reduce_scatter | solution.py:98
  325.3 0.9 slice.54
  326.3 0.9 copy.30
  327.2 0.7 slice.53
  327.9 0.7 slice.49
  328.6 0.6 pad_maximum_fusion.1
  (39 shorter events, 0.5 us)
Async XLA Ops:
  7.2 1.7 copy-start
  30.8 35.7 %all-to-all-start = ((bf16[16,12,4096]{2,1,0:T(8,128)(2,1)}), bf16[16,12,4096]{2,1,0:T(8,128)(2,1)S(1)}, u32[]{:S(2)}, u32[]{:S(2)}) async-start(bf16[16,12,4096]{2,1,0:T(8,128)(2,1)} %copy.22), calls=%async_computation | async-start | bytes 4194304 | tf_op jit(solution)/shard_map/all_to_all | solution.py:44
  42.2 28.9 %copy-start.8 = (s32[8,16]{1,0:T(8,128)S(1)}, s32[8,16]{1,0:T(8,128)}, u32[]{:S(2)}) copy-start(s32[8,16]{1,0:T(8,128)} %param.15) | copy-start | bytes 1540
  66.5 4.8 %copy-start.2 = (bf16[16,12,4096]{2,1,0:T(8,128)(2,1)}, bf16[16,12,4096]{2,1,0:T(8,128)(2,1)S(1)}, u32[]{:S(2)}) copy-start(bf16[16,12,4096]{2,1,0:T(8,128)(2,1)S(1)} %all-to-all-done) | copy-start | bytes 4718596
  66.5 29.9 %all-to-all-start.2 = ((bf16[16,12,4096]{2,1,0:T(8,128)(2,1)}), bf16[16,12,4096]{2,1,0:T(8,128)(2,1)}, u32[]{:S(2)}, u32[]{:S(2)}) async-start(bf16[16,12,4096]{2,1,0:T(8,128)(2,1)} %copy.26), calls=%async_computation.3 | async-start | bytes 4194304 | tf_op jit(solution)/shard_map/all_to_all | solution.py:44
  103.6 2.4 copy-start.3
  109.2 12.7 %copy-start.5 = (f32[8,16,1024]{2,1,0:T(8,128)S(1)}, f32[8,16,1024]{2,1,0:T(8,128)}, u32[]{:S(2)}) copy-start(f32[8,16,1024]{2,1,0:T(8,128)} %param.12) | copy-start | bytes 1572868
  109.2 12.7 %copy-start.6 = (f32[8,16,1024]{2,1,0:T(8,128)S(1)}, f32[8,16,1024]{2,1,0:T(8,128)}, u32[]{:S(2)}) copy-start(f32[8,16,1024]{2,1,0:T(8,128)} %param.13) | copy-start | bytes 1572868
  164.8 55.4 %all-to-all-start.3 = ((f32[16,12,4224]{2,1,0:T(8,128)}), f32[16,12,4224]{2,1,0:T(8,128)}, u32[]{:S(2)}, u32[]{:S(2)}) async-start(f32[16,12,4224]{2,1,0:T(8,128)} %reshape.165), calls=%async_computation.4 | async-start | bytes 8650752 | tf_op jit(solution)/shard_map/all_to_all | solution.py:78
  171.4 10.8 %copy-start.4 = (bf16[256,1024]{1,0:T(8,128)(2,1)S(1)}, bf16[256,1024]{1,0:T(8,128)(2,1)}, u32[]{:S(2)}) copy-start(bf16[256,1024]{1,0:T(8,128)(2,1)} %param.10) | copy-start | bytes 1572868
  200.1 29.2 %copy-start.7 = (s32[1,1,16,12]{2,1,3,0:T(1,128)S(1)}, s32[1,1,16,12]{2,1,3,0:T(1,128)}, u32[]{:S(2)}) copy-start(s32[1,1,16,12]{2,1,3,0:T(1,128)} %param.14) | copy-start | bytes 2308
  220.2 56.9 %all-to-all-start.1 = ((f32[16,12,4224]{2,1,0:T(8,128)}), f32[16,12,4224]{2,1,0:T(8,128)}, u32[]{:S(2)}, u32[]{:S(2)}) async-start(f32[16,12,4224]{2,1,0:T(8,128)} %reshape.156), calls=%async_computation.1 | async-start | bytes 8650752 | tf_op jit(solution)/shard_map/all_to_all | solution.py:78
  229.2 57.4 %reduce-scatter.5.cloned.1.call-start = ((), (), s32[]{:S(2)}) async-start(), calls=%async_computation.7 | async-start | bytes 1327104 | tf_op jit(solution)/shard_map/reduce_scatter | solution.py:98
  239.0 86.4 %reduce-scatter.3.cloned.1.call-start = ((), (), s32[]{:S(2)}) async-start(), calls=%async_computation.6 | async-start | bytes 1327104 | tf_op jit(solution)/shard_map/reduce_scatter | solution.py:98
  285.3 43.8 %copy-start.1 = (bf16[64,32,256]{2,1,0:T(8,128)(2,1)S(1)}, bf16[64,32,256]{2,1,0:T(8,128)(2,1)}, u32[]{:S(2)}) copy-start(bf16[64,32,256]{2,1,0:T(8,128)(2,1)} %param.9) | copy-start | bytes 3145732
Sparse Core Ops, SparseCore 0:
  239.1 36.7 reduce-scatter.4
  286.7 38.5 reduce-scatter.2

commit v2 on v1

v2 whole, which is shorter than its diff:
```python
import jax
import jax.numpy as jnp
from jax import lax
from jax.sharding import PartitionSpec as P

N_CHUNKS = 2
LANE = 128


def per_device(samples, basis, operators, cutouts, pixel_weights, detections, intersections):
    tiles_here, tile_cap, pixels = cutouts.shape
    coeff_dim = basis.shape[0]
    galaxy_count, sample_count, _unused = samples.shape
    sky_count = lax.axis_size("sky")
    expo_count = lax.axis_size("expo")
    send_cap = detections.shape[3]
    slot_count = sky_count * send_cap
    per_expo = sample_count // expo_count
    chunk_size = per_expo // N_CHUNKS
    chunk_samples = expo_count * chunk_size
    sent_rows = detections.reshape(sky_count, send_cap)
    positions = tiles_here * tile_cap
    block = chunk_size * coeff_dim
    like_width = slot_count // sky_count * chunk_size
    like_pad = -like_width % LANE

    arranged = samples.reshape(galaxy_count, expo_count, N_CHUNKS, chunk_size, coeff_dim)
    arranged = arranged.transpose(0, 2, 1, 3, 4).reshape(galaxy_count, N_CHUNKS, -1)
    send_index = jnp.maximum(sent_rows, 0).reshape(-1)
    live = intersections >= 0
    pick = jnp.maximum(intersections, 0).reshape(-1)
    target = jnp.where(live, intersections, slot_count).reshape(-1)
    holder = jnp.full((slot_count,), positions, jnp.int32)
    holder = holder.at[target].set(jnp.arange(positions, dtype=jnp.int32), mode="drop")

    listed_all = lax.all_gather(sent_rows, "expo", axis=0, tiled=False).reshape(-1)
    onehot = (listed_all[None, :] == jnp.arange(galaxy_count, dtype=jnp.int32)[:, None]).astype(
        jnp.float32
    )

    grad_pieces = []
    like_pieces = []
    for chunk in range(N_CHUNKS):
        sent = jnp.take(arranged[:, chunk], send_index, axis=0, mode="clip")
        sent = sent.reshape(sky_count, send_cap, chunk_samples * coeff_dim)
        incoming = lax.all_to_all(sent, "sky", split_axis=0, concat_axis=0, tiled=True)
        incoming = incoming.reshape(slot_count, chunk_samples * coeff_dim)
        picked = jnp.take(incoming, pick, axis=0, mode="clip").reshape(-1, coeff_dim)
        rendered = jnp.dot(picked, basis, preferred_element_type=jnp.float32).astype(jnp.bfloat16)
        rendered = rendered.reshape(tiles_here, tile_cap * chunk_samples, pixels)
        model = jnp.einsum("tnp,tpq->tnq", rendered, operators, preferred_element_type=jnp.float32)
        model = model.reshape(tiles_here, tile_cap, chunk_samples, pixels)
        resid = model - cutouts[:, :, None, :]
        weighted = pixel_weights[:, :, None, :] * resid
        pair_like = -0.5 / pixels * jnp.sum(weighted * resid, axis=-1)
        scaled = weighted.astype(jnp.bfloat16).reshape(tiles_here, tile_cap * chunk_samples, pixels)
        backed = jnp.einsum(
            "tnq,tpq->tnp", scaled, operators, preferred_element_type=jnp.float32
        ).astype(jnp.bfloat16)
        pair_grad = (
            -1.0
            / pixels
            * lax.dot_general(
                backed.reshape(-1, pixels),
                basis,
                (((1,), (1,)), ((), ())),
                preferred_element_type=jnp.float32,
            )
        )
        grad_rows = pair_grad.reshape(positions, expo_count, block).transpose(1, 0, 2)
        like_rows = pair_like.reshape(positions, expo_count, chunk_size).transpose(1, 0, 2)
        slot_grads = jnp.take(grad_rows, holder, axis=1, mode="fill", fill_value=0.0)
        slot_likes = jnp.take(like_rows, holder, axis=1, mode="fill", fill_value=0.0)
        send_back = jnp.concatenate(
            [
                slot_grads.reshape(expo_count, sky_count, send_cap * block),
                slot_likes.reshape(expo_count, sky_count, like_width),
                jnp.zeros((expo_count, sky_count, like_pad), jnp.float32),
            ],
            axis=2,
        ).reshape(expo_count * sky_count, -1)
        back = lax.all_to_all(
            send_back, ("expo", "sky"), split_axis=0, concat_axis=0, tiled=True
        )
        back_grads = back[:, : send_cap * block].reshape(-1, block)
        back_likes = back[:, send_cap * block : send_cap * block + like_width].reshape(
            -1, chunk_size
        )
        grads = jnp.dot(onehot, back_grads, precision=lax.Precision.HIGHEST)
        likes = jnp.dot(onehot, back_likes, precision=lax.Precision.HIGHEST)
        grad_pieces.append(grads.reshape(galaxy_count, chunk_size, coeff_dim))
        like_pieces.append(likes)
    grad_out = jnp.concatenate(grad_pieces, axis=1)
    like_out = jnp.concatenate(like_pieces, axis=1)
    return (like_out, grad_out)


def solution(mesh):
    placed = (
        P("sky", None, None),
        P(),
        P(("expo", "sky"), None, None),
        P(("expo", "sky"), None, None),
        P(("expo", "sky"), None, None),
        P("expo", "sky", None, None),
        P(("expo", "sky"), None),
    )
    return jax.shard_map(
        per_device,
        mesh=mesh,
        in_specs=placed,
        out_specs=(P("sky", "expo"), P("sky", "expo", None)),
        check_vma=False,
    )
```

time: 340 us -> 325 us (0.956)
  the two profiles are of different devices: /device:TPU:1 before, /device:TPU:21 now
where the time goes in v2:
time: 325 us; the launch traced here: 319 us
  local copies, waits for them, and re-layouts  110 us (34%)
  matrix products  70 us (22%)
  waiting for transfers between devices  49.9 us (15%)
  blocking collectives  44.4 us (14%)
  starting transfers between devices  37 us (11%)
  other arithmetic  6.22 us (2%)
    all_gather x1, blocking collectives, per_device(): lax.all_gather(sent_rows, 'expo', axis=0, tiled=False).reshape(-1)  44.4 us
    all_to_all x2, waiting for transfers between devices, per_device(): lax.all_to_all(sent, 'sky', split_axis=0, concat_axis=0, tiled=True)  36.1 us
    dot_general x2, matrix products, per_device(): jnp.einsum('tnp,tpq->tnq', rendered, operators, preferred_element_type=jn...  26.9 us
    all_to_all x2, starting transfers between devices, per_device(): lax.all_to_all(send_back, ('expo', 'sky'), split_axis=0, concat_axis=0, t...  23.1 us
    dot_general x2, matrix products, per_device(): jnp.einsum('tnq,tpq->tnp', scaled, operators, preferred_element_type=jnp....  22.1 us
    concatenate x7, local copies, waits for them, and re-layouts, per_device(): jnp.concatenate([slot_grads.reshape(expo_count, sky_count, send_cap * blo...  18.9 us
    all_to_all x2, starting transfers between devices, per_device(): lax.all_to_all(sent, 'sky', split_axis=0, concat_axis=0, tiled=True)  14 us
    all_to_all x2, local copies, waits for them, and re-layouts, per_device(): lax.all_to_all(send_back, ('expo', 'sky'), split_axis=0, concat_axis=0, t...  13.8 us
  transfers between devices with their start and end apart: 4, of which 3 were waited for; matrix products, arithmetic and copies ran while one was open for 13% of the time, Pallas kernels for 0%

profile of v2, /device:TPU:21, one launch (start us, length us, event | category | flops | bytes accessed | tf_op | source)
XLA Modules:
  0.0 319.1 jit_solution(8900417835878948766)
XLA Ops:
  0.6 1.5 reshape.167
  2.2 0.7 copy.51
  2.9 0.8 reshape.168
  4.1 1.5 gather_fusion.2
  5.6 1.5 reshape.177
  7.1 6.7 %all-to-all-start.2 = ((bf16[16,12,4096]{2,1,0:T(8,128)(2,1)}), bf16[16,12,4096]{2,1,0:T(8,128)(2,1)S(1)}, u32[]{:S(2)}, u32[]{:S(2)}) async-start(bf16[16,12,4096]{2,1,0:T(8,128)(2,1)} %reshape.177), calls=%async_computation.2 | async-start | bytes 4194304 | tf_op jit(solution)/shard_map/all_to_all | solution.py:46
  13.8 2.7 gather_fusion
  16.5 3.4 %reshape.169 = bf16[16,12,4096]{2,1,0:T(8,128)(2,1)} reshape(bf16[192,4096]{1,0:T(8,128)(2,1)} %gather_fusion) | data formatting | bytes 3145728 | tf_op jit(solution)/shard_map/reshape | solution.py:45
  19.9 19.1 %all-to-all-done.2 = bf16[16,12,4096]{2,1,0:T(8,128)(2,1)S(1)} async-done(((bf16[16,12,4096]{2,1,0:T(8,128)(2,1)}), bf16[16,12,4096]{2,1,0:T(8,128)(2,1)S(1)}, u32[]{:S(2)}, u32[]{:S(2)}) %all-to-all-start.2) | async-done | bytes 1572896 | tf_op jit(solution)/shard_map/all_to_all | solution.py:46
  38.9 7.3 %all-to-all-start = ((bf16[16,12,4096]{2,1,0:T(8,128)(2,1)}), bf16[16,12,4096]{2,1,0:T(8,128)(2,1)}, u32[]{:S(2)}, u32[]{:S(2)}) async-start(bf16[16,12,4096]{2,1,0:T(8,128)(2,1)} %reshape.169), calls=%async_computation | async-start | bytes 4194304 | tf_op jit(solution)/shard_map/all_to_all | solution.py:46
  46.4 1.2 scatter_custom_fusion
  47.7 2.5 reshape.178
  50.1 2.2 gather_fusion.3
  52.3 1.6 reshape.179
  53.9 17.1 %all-to-all-done = bf16[16,12,4096]{2,1,0:T(8,128)(2,1)} async-done(((bf16[16,12,4096]{2,1,0:T(8,128)(2,1)}), bf16[16,12,4096]{2,1,0:T(8,128)(2,1)}, u32[]{:S(2)}, u32[]{:S(2)}) %all-to-all-start) | async-done | bytes 1572896 | tf_op jit(solution)/shard_map/all_to_all | solution.py:46
  70.9 2.5 reshape.170
  73.4 2.2 gather_fusion.1
  75.6 1.6 reshape.171
  77.1 1.3 convolution_convert_fusion
  78.4 3.2 %convolution_convert_fusion.1 = bf16[2048,1024]{1,0:T(8,128)(2,1)} fusion(bf16[2048,256]{1,0:T(8,128)(2,1)S(1)} %reshape.171, bf16[256,1024]{1,0:T(8,128)(2,1)S(1)} %copy-done), kind=kOutput, calls=%fused_computation.20 | convolution fusion | flops 1075838976 | bytes 5767168 | tf_op jit(solution)/shard_map/dot_general | solution.py:49
  81.6 12.7 %fusion.20 = f32[8,256,1024]{2,1,0:T(8,128)} fusion(bf16[8,256,1024]{2,1,0:T(8,128)(2,1)S(1)} %bitcast.96, bf16[8,1024,1024]{2,1,0:T(8,128)(2,1)} %param.13), kind=kOutput, calls=%fused_computation.60 | convolution fusion | flops 4294967296 | bytes 29360128 | tf_op jit(solution)/shard_map/tnp,tpq->tnq/dot_general | solution.py:51
  94.3 14.1 %fusion.5 = (f32[8,256]{1,0:T(8,128)S(1)}, f32[8,256]{1,0:T(8,128)S(1)}, bf16[8,256,1024]{2,1,0:T(8,128)(2,1)}, bf16[8,256,1024]{2,1,0:T(8,128)(2,1)}) fusion(f32[8,16,1024]{2,1,0:T(8,128)S(1)} %copy-done.3, f32[8,16,1024]{2,1,0:T(8,128)S(1)} %copy-done.4, f32[8,256,1024]{2,1,0:T(8,128)} %fusion.20, bf16[8,256,1024]{2,1,0:T(8,128)(2,1)} %bitcast.95, ...), kind=kOutput, calls=%fused_computation.18 | convolution fusion | flops 4315934720 | bytes 38813696 | tf_op jit(solution)/shard_map/tnp,tpq->tnq/dot_general | solution.py:51
  108.5 11.2 %convolution_convert_fusion.2 = bf16[8,256,1024]{2,1,0:T(8,128)(2,1)} fusion(bf16[8,256,1024]{2,1,0:T(8,128)(2,1)} %get-tuple-element.15, bf16[8,1024,1024]{2,1,0:T(8,128)(2,1)} %param.13), kind=kOutput, calls=%fused_computation.27 | convolution fusion | flops 4297064448 | bytes 25165824 | tf_op jit(solution)/shard_map/tnq,tpq->tnp/dot_general | solution.py:57
  119.7 4.8 %convolution_multiply_fusion = f32[2048,256]{1,0:T(8,128)} fusion(bf16[2048,1024]{1,0:T(8,128)(2,1)} %bitcast.112, bf16[256,1024]{1,0:T(8,128)(2,1)S(1)} %copy-done), kind=kOutput, calls=%fused_computation.25 | convolution fusion | flops 1074266112 | bytes 6815744 | tf_op jit(solution)/shard_map/dot_general | solution.py:63
  124.5 1.9 reshape.182
  126.4 10.8 %convolution_convert_fusion.3 = bf16[8,256,1024]{2,1,0:T(8,128)(2,1)} fusion(bf16[8,256,1024]{2,1,0:T(8,128)(2,1)} %get-tuple-element.14, bf16[8,1024,1024]{2,1,0:T(8,128)(2,1)} %param.13), kind=kOutput, calls=%fused_computation.28 | convolution fusion | flops 4297064448 | bytes 25165824 | tf_op jit(solution)/shard_map/tnq,tpq->tnp/dot_general | solution.py:57
  137.2 4.8 %convolution_multiply_fusion.1 = f32[2048,256]{1,0:T(8,128)} fusion(bf16[2048,1024]{1,0:T(8,128)(2,1)} %bitcast.113, bf16[256,1024]{1,0:T(8,128)(2,1)S(1)} %copy-done), kind=kOutput, calls=%fused_computation.26 | convolution fusion | flops 1074266112 | bytes 6815744 | tf_op jit(solution)/shard_map/dot_general | solution.py:63
  142.1 2.9 reshape.174
  145.0 2.5 gather_fusion.6
  147.5 4.0 %gather_fusion.4 = f32[192,8,512]{2,1,0:T(8,128)} fusion(f32[8,128,512]{2,0,1:T(8,128)} %bitcast.98, s32[1024]{0:T(1024)S(1)} %pad_clamp_fusion), kind=kCustom, calls=%fused_computation.clone | custom fusion | bytes 6292224 | tf_op jit(solution)/shard_map/jit(_take)/gather | solution.py:72
  151.5 5.0 %select_bitcast_fusion.1 = (f32[8,192,512]{2,0,1:T(8,128)S(1)}, f32[8,192,512]{2,0,1:T(8,128)}) fusion(f32[192,8,512]{2,1,0:T(8,128)} %gather_fusion.4, pred[192]{0:T(512)(128)(4,1)S(1)} %compare_and_fusion, f32[192,8,512]{2,1,0:T(8,128)} %gather_fusion.6), kind=kLoop, calls=%fused_computation.24 | loop fusion | flops 1572864 | bytes 12583104 | tf_op jit(solution)/shard_map/jit(_take)/select_n | solution.py:72
  156.5 3.4 %copy.34 = f32[8,192,512]{2,1,0:T(8,128)} copy(f32[8,192,512]{2,0,1:T(8,128)S(1)} %get-tuple-element.20) | data formatting | bytes 6291456 | tf_op jit(solution)/shard_map/jit(_take)/select_n | solution.py:72
  160.0 5.0 %concatenate.24 = f32[128,6144]{1,0:T(8,128)} reshape(f32[8,192,512]{2,1,0:T(8,128)} %copy.34) | data formatting | bytes 6291456 | tf_op jit(solution)/shard_map/concatenate | solution.py:74
  165.0 0.5 mul.54
  165.4 0.8 copy.35
  166.3 0.9 gather_fusion.5
  167.4 1.2 copy.36
  168.9 4.3 %concatenate.27 = f32[128,6272]{1,0:T(8,128)} concatenate(f32[128,6144]{1,0:T(8,128)} %concatenate.24, f32[128,24]{1,0:T(8,128)S(1)} %concatenate.25, f32[128,104]{1,0:T(8,128)S(1)} %concatenate.26), dimensions={1} | concatenate | bytes 6422528 | tf_op jit(solution)/shard_map/concatenate | solution.py:74
  173.2 6.9 %copy.37 = f32[128,1,6272]{2,1,0:T(1,128)} copy(f32[128,1,6272]{2,0,1:T(8,128)} %bitcast.100) | data formatting | bytes 6422528 | tf_op jit(solution)/shard_map/all_to_all | solution.py:82
  180.1 13.9 %all-to-all-start.1 = ((f32[128,1,6272]{2,1,0:T(1,128)}), f32[128,1,6272]{2,1,0:T(1,128)}, u32[]{:S(2)}, u32[]{:S(2)}) async-start(f32[128,1,6272]{2,1,0:T(1,128)} %copy.37), calls=%async_computation.1 | async-start | bytes 6422528 | tf_op jit(solution)/shard_map/all_to_all | solution.py:82
  194.0 5.4 %copy.38 = f32[8,192,512]{2,1,0:T(8,128)} copy(f32[8,192,512]{2,0,1:T(8,128)} %get-tuple-element.21) | data formatting | bytes 6291456 | tf_op jit(solution)/shard_map/jit(_take)/select_n | solution.py:72
  199.4 4.8 %concatenate.28 = f32[128,6144]{1,0:T(8,128)} reshape(f32[8,192,512]{2,1,0:T(8,128)} %copy.38) | data formatting | bytes 6291456 | tf_op jit(solution)/shard_map/concatenate | solution.py:74
  204.3 0.5 mul.59
  204.7 0.9 gather_fusion.7
  206.3 4.3 %concatenate.30 = f32[128,6272]{1,0:T(8,128)} concatenate(f32[128,6144]{1,0:T(8,128)} %concatenate.28, f32[128,24]{1,0:T(8,128)S(1)} %concatenate.29, f32[128,104]{1,0:T(8,128)S(1)} %concatenate.26), dimensions={1} | concatenate | bytes 6422528 | tf_op jit(solution)/shard_map/concatenate | solution.py:74
  210.6 6.9 %copy.40 = f32[128,1,6272]{2,1,0:T(1,128)} copy(f32[128,1,6272]{2,0,1:T(8,128)} %bitcast.99) | data formatting | bytes 6422528 | tf_op jit(solution)/shard_map/all_to_all | solution.py:82
  217.5 13.8 %all-to-all-done.1 = f32[128,1,6272]{2,1,0:T(1,128)} async-done(((f32[128,1,6272]{2,1,0:T(1,128)}), f32[128,1,6272]{2,1,0:T(1,128)}, u32[]{:S(2)}, u32[]{:S(2)}) %all-to-all-start.1) | async-done | bytes 3211296 | tf_op jit(solution)/shard_map/all_to_all | solution.py:82
  231.3 9.2 %all-to-all-start.3 = ((f32[128,1,6272]{2,1,0:T(1,128)}), f32[128,1,6272]{2,1,0:T(1,128)}, u32[]{:S(2)}, u32[]{:S(2)}) async-start(f32[128,1,6272]{2,1,0:T(1,128)} %copy.40), calls=%async_computation.3 | async-start | bytes 6422528 | tf_op jit(solution)/shard_map/all_to_all | solution.py:82
  240.5 44.4 %all-gather = s32[8,1,16,12]{2,1,3,0:T(1,128)S(1)} all-gather(s32[1,1,16,12]{2,1,3,0:T(1,128)S(1)} %copy-done.5), channel_id=2, replica_groups=mesh['expo'=8,'sky'=16] {'expo'}, dimensions={0}, use_global_device_ids=true | all-gather | bytes 6912 | tf_op jit(solution)/shard_map/all_gather | solution.py:36
  285.1 2.1 copy.50
  287.2 2.0 slice.44
  289.2 2.1 copy.49
  291.4 1.9 slice.45
  293.3 4.8 %reshape.184 = f32[1536,512]{1,0:T(8,128)} reshape(f32[128,6144]{1,0:T(8,128)} %slice.44) | data formatting | bytes 6291456 | tf_op jit(solution)/shard_map/reshape | solution.py:85
  298.1 3.6 %copy.41 = f32[512,1536]{1,0:T(8,128)} copy(f32[512,1536]{0,1:T(8,128)} %bitcast.107) | data formatting | bytes 6291456 | tf_op jit(solution)/shard_map/dot_general | solution.py:89
  301.6 4.6 %reshape.185 = f32[1536,512]{1,0:T(8,128)} reshape(f32[128,6144]{1,0:T(8,128)} %slice.45) | data formatting | bytes 6291456 | tf_op jit(solution)/shard_map/reshape | solution.py:85
  306.2 3.5 %copy.42 = f32[512,1536]{1,0:T(8,128)} copy(f32[512,1536]{0,1:T(8,128)} %bitcast.108) | data formatting | bytes 6291456 | tf_op jit(solution)/shard_map/dot_general | solution.py:89
  309.7 3.8 %fusion.11 = f32[64,2,256]{2,0,1:T(8,128)S(1)} fusion(f32[2,256,1536]{2,1,0:T(8,128)} %bitcast.105, s32[1536]{0:T(1024)S(1)} %eq.15), kind=kOutput, calls=%fused_computation.38 | convolution fusion | flops 604078080 | bytes 3282944 | tf_op jit(solution)/shard_map/dot_general | solution.py:89
  313.5 1.8 fusion.9
  315.3 0.9 copy.43
  316.5 0.7 fusion.8
  317.2 0.3 reshape.183
  317.5 0.7 fusion.7
  318.2 0.6 pad_maximum_fusion.1
  (42 shorter events, 2.2 us)
Async XLA Ops:
  0.6 76.5 %copy-start = (bf16[256,1024]{1,0:T(8,128)(2,1)S(1)}, bf16[256,1024]{1,0:T(8,128)(2,1)}, u32[]{:S(2)}) copy-start(bf16[256,1024]{1,0:T(8,128)(2,1)} %param.12) | copy-start | bytes 1572868
  2.2 1.7 copy-start.5
  7.1 31.8 %all-to-all-start.2 = ((bf16[16,12,4096]{2,1,0:T(8,128)(2,1)}), bf16[16,12,4096]{2,1,0:T(8,128)(2,1)S(1)}, u32[]{:S(2)}, u32[]{:S(2)}) async-start(bf16[16,12,4096]{2,1,0:T(8,128)(2,1)} %reshape.177), calls=%async_computation.2 | async-start | bytes 4194304 | tf_op jit(solution)/shard_map/all_to_all | solution.py:46
  16.5 29.8 %copy-start.6 = (s32[8,16]{1,0:T(8,128)S(1)}, s32[8,16]{1,0:T(8,128)}, u32[]{:S(2)}) copy-start(s32[8,16]{1,0:T(8,128)} %param.17) | copy-start | bytes 1540
  38.9 8.7 %copy-start.2 = (bf16[16,12,4096]{2,1,0:T(8,128)(2,1)}, bf16[16,12,4096]{2,1,0:T(8,128)(2,1)S(1)}, u32[]{:S(2)}) copy-start(bf16[16,12,4096]{2,1,0:T(8,128)(2,1)S(1)} %all-to-all-done.2) | copy-start | bytes 4718596
  38.9 32.0 %all-to-all-start = ((bf16[16,12,4096]{2,1,0:T(8,128)(2,1)}), bf16[16,12,4096]{2,1,0:T(8,128)(2,1)}, u32[]{:S(2)}, u32[]{:S(2)}) async-start(bf16[16,12,4096]{2,1,0:T(8,128)(2,1)} %reshape.169), calls=%async_computation | async-start | bytes 4194304 | tf_op jit(solution)/shard_map/all_to_all | solution.py:46
  81.6 12.7 %copy-start.3 = (f32[8,16,1024]{2,1,0:T(8,128)S(1)}, f32[8,16,1024]{2,1,0:T(8,128)}, u32[]{:S(2)}) copy-start(f32[8,16,1024]{2,1,0:T(8,128)} %param.14) | copy-start | bytes 1572868
  81.6 12.7 %copy-start.4 = (f32[8,16,1024]{2,1,0:T(8,128)S(1)}, f32[8,16,1024]{2,1,0:T(8,128)}, u32[]{:S(2)}) copy-start(f32[8,16,1024]{2,1,0:T(8,128)} %param.15) | copy-start | bytes 1572868
  180.1 51.2 %all-to-all-start.1 = ((f32[128,1,6272]{2,1,0:T(1,128)}), f32[128,1,6272]{2,1,0:T(1,128)}, u32[]{:S(2)}, u32[]{:S(2)}) async-start(f32[128,1,6272]{2,1,0:T(1,128)} %copy.37), calls=%async_computation.1 | async-start | bytes 6422528 | tf_op jit(solution)/shard_map/all_to_all | solution.py:82
  231.3 57.9 %all-to-all-start.3 = ((f32[128,1,6272]{2,1,0:T(1,128)}), f32[128,1,6272]{2,1,0:T(1,128)}, u32[]{:S(2)}, u32[]{:S(2)}) async-start(f32[128,1,6272]{2,1,0:T(1,128)} %copy.40), calls=%async_computation.3 | async-start | bytes 6422528 | tf_op jit(solution)/shard_map/all_to_all | solution.py:82
  309.7 3.8 %copy-start.1 = (f32[512,1536]{1,0:T(8,128)S(1)}, f32[512,1536]{1,0:T(8,128)}, u32[]{:S(2)}) copy-start(f32[512,1536]{1,0:T(8,128)} %copy.42) | copy-start | bytes 9437188

commit v3 on v2

v3 whole, which is shorter than its diff:
```python
import jax
import jax.numpy as jnp
from jax import lax
from jax.sharding import PartitionSpec as P

N_CHUNKS = 2
LANE = 128


def per_device(samples, basis, operators, cutouts, pixel_weights, detections, intersections):
    tiles_here, tile_cap, pixels = cutouts.shape
    coeff_dim = basis.shape[0]
    galaxy_count, sample_count, _unused = samples.shape
    sky_count = lax.axis_size("sky")
    expo_count = lax.axis_size("expo")
    send_cap = detections.shape[3]
    slot_count = sky_count * send_cap
    per_expo = sample_count // expo_count
    chunk_size = per_expo // N_CHUNKS
    chunk_samples = expo_count * chunk_size
    positions = tiles_here * tile_cap
    devices = expo_count * sky_count

    listed_all = lax.all_gather(
        detections.reshape(sky_count, send_cap), "expo", axis=0, tiled=False
    )
    sent_rows = lax.dynamic_index_in_dim(listed_all, lax.axis_index("expo"), 0, keepdims=False)
    listed_flat = listed_all.reshape(-1)
    onehot = (listed_flat[None, :] == jnp.arange(galaxy_count, dtype=jnp.int32)[:, None]).astype(
        jnp.float32
    )
    onehot_k = (
        onehot[:, None, :, None]
        * jnp.eye(chunk_size, dtype=jnp.float32)[None, :, None, :]
    ).reshape(galaxy_count * chunk_size, -1)

    arranged = samples.reshape(galaxy_count, expo_count, N_CHUNKS, chunk_size, coeff_dim)
    arranged = arranged.transpose(2, 0, 1, 3, 4).reshape(N_CHUNKS, -1, coeff_dim)
    sample_ids = jnp.arange(chunk_samples, dtype=jnp.int32)
    send_index = (jnp.maximum(sent_rows, 0).reshape(-1, 1) * chunk_samples + sample_ids).reshape(-1)
    live = intersections >= 0
    pick = jnp.maximum(intersections, 0).reshape(-1)
    pick_index = (pick.reshape(-1, 1) * chunk_samples + sample_ids).reshape(-1)
    target = jnp.where(live, intersections, slot_count).reshape(-1)
    holder = jnp.full((slot_count,), positions, jnp.int32)
    holder = holder.at[target].set(jnp.arange(positions, dtype=jnp.int32), mode="drop")
    expo_ids = jnp.arange(expo_count, dtype=jnp.int32)
    k_ids = jnp.arange(chunk_size, dtype=jnp.int32)
    back_index = (
        (holder[None, :, None] * expo_count + expo_ids[:, None, None]) * chunk_size
        + k_ids[None, None, :]
    )
    back_index = jnp.where(holder[None, :, None] < positions, back_index, positions * chunk_samples)
    back_index = back_index.reshape(-1)

    grad_pieces = []
    like_rows = []
    for chunk in range(N_CHUNKS):
        sent = jnp.take(arranged[chunk], send_index, axis=0, mode="clip")
        incoming = lax.all_to_all(sent, "sky", split_axis=0, concat_axis=0, tiled=True)
        picked = jnp.take(incoming, pick_index, axis=0, mode="clip")
        rendered = jnp.dot(picked, basis, preferred_element_type=jnp.float32).astype(jnp.bfloat16)
        rendered = rendered.reshape(tiles_here, tile_cap * chunk_samples, pixels)
        model = jnp.einsum("tnp,tpq->tnq", rendered, operators, preferred_element_type=jnp.float32)
        model = model.reshape(tiles_here, tile_cap, chunk_samples, pixels)
        resid = model - cutouts[:, :, None, :]
        weighted = pixel_weights[:, :, None, :] * resid
        pair_like = -0.5 / pixels * jnp.sum(weighted * resid, axis=-1)
        scaled = weighted.astype(jnp.bfloat16).reshape(tiles_here, tile_cap * chunk_samples, pixels)
        backed = jnp.einsum(
            "tnq,tpq->tnp", scaled, operators, preferred_element_type=jnp.float32
        ).astype(jnp.bfloat16)
        pair_grad = (
            -1.0
            / pixels
            * lax.dot_general(
                backed.reshape(-1, pixels),
                basis,
                (((1,), (1,)), ((), ())),
                preferred_element_type=jnp.float32,
            )
        )
        send_back = jnp.take(pair_grad, back_index, axis=0, mode="fill", fill_value=0.0)
        back = lax.all_to_all(send_back, ("expo", "sky"), split_axis=0, concat_axis=0, tiled=True)
        grads = jnp.dot(onehot_k, back, precision=lax.Precision.HIGHEST)
        grad_pieces.append(grads.reshape(galaxy_count, chunk_size, coeff_dim))
        like_rows.append(pair_like.reshape(positions, expo_count, chunk_size))
    likes = jnp.stack(like_rows, axis=2).reshape(positions, expo_count, per_expo)
    likes = jnp.take(likes.transpose(1, 0, 2), holder, axis=1, mode="fill", fill_value=0.0)
    like_width = send_cap * per_expo
    likes = likes.reshape(devices, like_width)
    likes = jnp.pad(likes, ((0, 0), (0, -like_width % LANE)))
    back_likes = lax.all_to_all(likes, ("expo", "sky"), split_axis=0, concat_axis=0, tiled=True)
    back_likes = back_likes[:, :like_width].reshape(-1, per_expo)
    like_out = jnp.dot(onehot, back_likes, precision=lax.Precision.HIGHEST)
    grad_out = jnp.concatenate(grad_pieces, axis=1)
    return (like_out, grad_out)


def solution(mesh):
    placed = (
        P("sky", None, None),
        P(),
        P(("expo", "sky"), None, None),
        P(("expo", "sky"), None, None),
        P(("expo", "sky"), None, None),
        P("expo", "sky", None, None),
        P(("expo", "sky"), None),
    )
    return jax.shard_map(
        per_device,
        mesh=mesh,
        in_specs=placed,
        out_specs=(P("sky", "expo"), P("sky", "expo", None)),
        check_vma=False,
    )
```

time: 325 us -> 305 us (0.938)
  the two profiles are of different devices: /device:TPU:21 before, /device:TPU:1 now
where the time goes in v3:
time: 305 us; the launch traced here: 304 us
  local copies, waits for them, and re-layouts  81 us (27%)
  matrix products  70 us (23%)
  blocking collectives  62.3 us (20%)
  waiting for transfers between devices  58.2 us (19%)
  starting transfers between devices  25.2 us (8%)
  other arithmetic  6.39 us (2%)
    all_to_all x1, blocking collectives, per_device(): lax.all_to_all(send_back, ('expo', 'sky'), split_axis=0, concat_axis=0, t...  46.6 us
    all_to_all x1, waiting for transfers between devices, per_device(): lax.all_to_all(send_back, ('expo', 'sky'), split_axis=0, concat_axis=0, t...  32.8 us
    dot_general x2, matrix products, per_device(): jnp.einsum('tnp,tpq->tnq', rendered, operators, preferred_element_type=jn...  26.8 us
    gather x2, local copies, waits for them, and re-layouts, per_device(): jnp.take(pair_grad, back_index, axis=0, mode='fill', fill_value=0.0)  26.2 us
    gather x2, local copies, waits for them, and re-layouts, per_device(): sent = jnp.take(arranged[chunk], send_index, axis=0, mode='clip')  25.9 us
    dot_general x2, matrix products, per_device(): jnp.einsum('tnq,tpq->tnp', scaled, operators, preferred_element_type=jnp....  21.7 us
    all_to_all x2, waiting for transfers between devices, per_device(): lax.all_to_all(sent, 'sky', split_axis=0, concat_axis=0, tiled=True)  21.1 us
    gather x2, local copies, waits for them, and re-layouts, per_device(): picked = jnp.take(incoming, pick_index, axis=0, mode='clip')  15.7 us
  transfers between devices with their start and end apart: 4, of which 4 were waited for; matrix products, arithmetic and copies ran while one was open for 12% of the time, Pallas kernels for 0%

profile of v3, /device:TPU:1, one launch (start us, length us, event | category | flops | bytes accessed | tf_op | source)
XLA Modules:
  0.0 304.0 jit_solution(10062515882974735889)
XLA Ops:
  0.6 0.0 copy-start
  0.6 15.7 %all-gather = s32[8,1,16,12]{2,1,3,0:T(1,128)S(1)} all-gather(s32[1,1,16,12]{2,1,3,0:T(1,128)} %param.14), channel_id=2, replica_groups=mesh['expo'=8,'sky'=16] {'expo'}, dimensions={0}, use_global_device_ids=true | all-gather | bytes 6912 | tf_op jit(solution)/shard_map/all_gather | solution.py:24
  16.4 0.1 copy.28
  16.5 0.1 mul.137
  16.6 0.1 iota_add_fusion
  16.7 0.1 reshape.308
  16.8 1.5 reshape.283
  18.2 0.7 copy.37
  19.0 0.7 fusion.21
  19.7 0.2 squeeze.9
  19.9 12.9 %gather_fusion.2 = bf16[3072,256]{1,0:T(8,128)(2,1)} fusion(bf16[1024,256]{1,0:T(8,128)(2,1)S(1)} %squeeze.9, s32[3072]{0:T(1024)S(1)} %broadcast_clamp_fusion), kind=kCustom, calls=%fused_computation.4 | custom fusion | bytes 3158016 | tf_op jit(solution)/shard_map/jit(_take)/gather | solution.py:59
  32.9 6.8 %all-to-all-start.1 = ((bf16[16,192,256]{2,1,0:T(8,128)(2,1)}), bf16[16,192,256]{2,1,0:T(8,128)(2,1)S(1)}, u32[]{:S(2)}, u32[]{:S(2)}) async-start(bf16[16,192,256]{2,1,0:T(8,128)(2,1)} %bitcast.89), calls=%async_computation.1 | async-start | bytes 3145728 | tf_op jit(solution)/shard_map/all_to_all | solution.py:60
  39.6 0.1 mul.140
  39.7 0.1 iota_add_fusion.1
  39.8 0.1 reshape.316
  39.9 0.2 squeeze.8
  40.1 13.0 %gather_fusion = bf16[3072,256]{1,0:T(8,128)(2,1)} fusion(bf16[1024,256]{1,0:T(8,128)(2,1)S(1)} %squeeze.8, s32[3072]{0:T(1024)S(1)} %broadcast_clamp_fusion), kind=kCustom, calls=%fused_computation.2 | custom fusion | bytes 3158016 | tf_op jit(solution)/shard_map/jit(_take)/gather | solution.py:59
  53.1 0.1 reshape.282
  53.2 1.0 scatter_custom_fusion
  54.1 8.8 %all-to-all-done.1 = bf16[16,192,256]{2,1,0:T(8,128)(2,1)S(1)} async-done(((bf16[16,192,256]{2,1,0:T(8,128)(2,1)}), bf16[16,192,256]{2,1,0:T(8,128)(2,1)S(1)}, u32[]{:S(2)}, u32[]{:S(2)}) %all-to-all-start.1) | async-done | bytes 1572896 | tf_op jit(solution)/shard_map/all_to_all | solution.py:60
  62.9 4.6 %all-to-all-start = ((bf16[16,192,256]{2,1,0:T(8,128)(2,1)}), bf16[16,192,256]{2,1,0:T(8,128)(2,1)}, u32[]{:S(2)}, u32[]{:S(2)}) async-start(bf16[16,192,256]{2,1,0:T(8,128)(2,1)} %bitcast.88), calls=%async_computation | async-start | bytes 3145728 | tf_op jit(solution)/shard_map/all_to_all | solution.py:60
  67.5 0.3 add_select_fusion
  67.8 0.4 select_n.53
  68.2 7.5 %gather_fusion.3 = bf16[2048,256]{1,0:T(8,128)(2,1)S(1)} fusion(bf16[3072,256]{1,0:T(8,128)(2,1)S(1)} %bitcast.82, s32[2048]{0:T(1024)S(1)} %broadcast_clamp_fusion.1), kind=kCustom, calls=%fused_computation.5 | custom fusion | bytes 2105344 | tf_op jit(solution)/shard_map/jit(_take)/gather | solution.py:61
  75.8 12.3 %all-to-all-done = bf16[16,192,256]{2,1,0:T(8,128)(2,1)} async-done(((bf16[16,192,256]{2,1,0:T(8,128)(2,1)}), bf16[16,192,256]{2,1,0:T(8,128)(2,1)}, u32[]{:S(2)}, u32[]{:S(2)}) %all-to-all-start) | async-done | bytes 1572896 | tf_op jit(solution)/shard_map/all_to_all | solution.py:60
  88.1 8.2 %gather_fusion.1 = bf16[2048,256]{1,0:T(8,128)(2,1)S(1)} fusion(bf16[3072,256]{1,0:T(8,128)(2,1)} %bitcast.4, s32[2048]{0:T(1024)S(1)} %broadcast_clamp_fusion.1), kind=kCustom, calls=%fused_computation.3 | custom fusion | bytes 2105344 | tf_op jit(solution)/shard_map/jit(_take)/gather | solution.py:61
  96.4 1.3 convolution_convert_fusion
  97.6 3.2 %convolution_convert_fusion.1 = bf16[2048,1024]{1,0:T(8,128)(2,1)} fusion(bf16[2048,256]{1,0:T(8,128)(2,1)S(1)} %gather_fusion.1, bf16[256,1024]{1,0:T(8,128)(2,1)S(1)} %copy-done), kind=kOutput, calls=%fused_computation.19 | convolution fusion | flops 1075838976 | bytes 5767168 | tf_op jit(solution)/shard_map/dot_general | solution.py:62
  100.8 12.7 %fusion.22 = f32[8,256,1024]{2,1,0:T(8,128)} fusion(bf16[8,256,1024]{2,1,0:T(8,128)(2,1)S(1)} %bitcast.84, bf16[8,1024,1024]{2,1,0:T(8,128)(2,1)} %param.11), kind=kOutput, calls=%fused_computation.67 | convolution fusion | flops 4294967296 | bytes 29360128 | tf_op jit(solution)/shard_map/tnp,tpq->tnq/dot_general | solution.py:64
  113.5 14.1 %fusion.5 = (f32[8,256]{1,0:T(8,128)S(1)}, f32[8,256]{1,0:T(8,128)S(1)}, bf16[8,256,1024]{2,1,0:T(8,128)(2,1)}, bf16[8,256,1024]{2,1,0:T(8,128)(2,1)}) fusion(f32[8,16,1024]{2,1,0:T(8,128)S(1)} %copy-done.1, f32[8,16,1024]{2,1,0:T(8,128)S(1)} %copy-done.2, f32[8,256,1024]{2,1,0:T(8,128)} %fusion.22, bf16[8,256,1024]{2,1,0:T(8,128)(2,1)} %bitcast.83, ...), kind=kOutput, calls=%fused_computation.17 | convolution fusion | flops 4315934720 | bytes 38813696 | tf_op jit(solution)/shard_map/tnp,tpq->tnq/dot_general | solution.py:64
  127.7 10.8 %convolution_convert_fusion.3 = bf16[8,256,1024]{2,1,0:T(8,128)(2,1)} fusion(bf16[8,256,1024]{2,1,0:T(8,128)(2,1)} %get-tuple-element.13, bf16[8,1024,1024]{2,1,0:T(8,128)(2,1)} %param.11), kind=kOutput, calls=%fused_computation.23 | convolution fusion | flops 4297064448 | bytes 25165824 | tf_op jit(solution)/shard_map/tnq,tpq->tnp/dot_general | solution.py:70
  138.5 3.5 %convolution_multiply_fusion.1 = f32[2048,256]{1,0:T(8,128)S(1)} fusion(bf16[2048,1024]{1,0:T(8,128)(2,1)} %bitcast.95, bf16[256,1024]{1,0:T(8,128)(2,1)S(1)} %copy-done), kind=kOutput, calls=%fused_computation.21 | convolution fusion | flops 1074266112 | bytes 6815744 | tf_op jit(solution)/shard_map/dot_general | solution.py:76
  142.0 10.8 %convolution_convert_fusion.2 = bf16[8,256,1024]{2,1,0:T(8,128)(2,1)} fusion(bf16[8,256,1024]{2,1,0:T(8,128)(2,1)} %get-tuple-element.14, bf16[8,1024,1024]{2,1,0:T(8,128)(2,1)} %param.11), kind=kOutput, calls=%fused_computation.22 | convolution fusion | flops 4297064448 | bytes 25165824 | tf_op jit(solution)/shard_map/tnq,tpq->tnp/dot_general | solution.py:70
  152.8 4.8 %convolution_multiply_fusion = f32[2048,256]{1,0:T(8,128)} fusion(bf16[2048,1024]{1,0:T(8,128)(2,1)} %bitcast.96, bf16[256,1024]{1,0:T(8,128)(2,1)S(1)} %copy-done), kind=kOutput, calls=%fused_computation.20 | convolution fusion | flops 1074266112 | bytes 6815744 | tf_op jit(solution)/shard_map/dot_general | solution.py:76
  157.7 12.4 %gather_fusion.5 = f32[3072,256]{1,0:T(8,128)} fusion(f32[2048,256]{1,0:T(8,128)S(1)} %convolution_multiply_fusion.1, s32[3072]{0:T(1024)S(1)} %fusion.17), kind=kCustom, calls=%fused_computation.clone | custom fusion | bytes 6303744 | tf_op jit(solution)/shard_map/jit(_take)/gather | solution.py:83
  170.0 13.9 %gather_fusion.6 = f32[3072,256]{1,0:T(8,128)} fusion(f32[2048,256]{1,0:T(8,128)} %convolution_multiply_fusion, s32[3072]{0:T(1024)S(1)} %fusion.17), kind=kCustom, calls=%fused_computation.1.clone | custom fusion | bytes 6303744 | tf_op jit(solution)/shard_map/jit(_take)/gather | solution.py:83
  183.9 0.5 mul.144
  184.4 0.2 copy.29
  184.6 0.5 mul.148
  185.1 0.2 copy.30
  185.3 0.2 copy.31
  185.5 0.9 gather_fusion.4
  186.4 0.3 select_bitcast_fusion
  186.6 1.2 copy.32
  187.8 0.3 select_n.51
  188.1 0.6 pad.4
  188.7 8.8 %all-to-all-start.2 = ((f32[128,1,128]{2,1,0:T(1,128)}), f32[128,1,128]{2,1,0:T(1,128)S(1)}, u32[]{:S(2)}, u32[]{:S(2)}) async-start(f32[128,1,128]{2,1,0:T(1,128)} %bitcast.14), calls=%async_computation.2 | async-start | bytes 131072 | tf_op jit(solution)/shard_map/all_to_all | solution.py:93
  197.5 5.3 %broadcast_select_fusion.1 = (f32[3072,256]{1,0:T(8,128)}, f32[3072,256]{1,0:T(8,128)}) fusion(f32[3072,256]{1,0:T(8,128)} %gather_fusion.5, pred[3072]{0:T(1024)(128)(4,1)S(1)} %compare_and_fusion, f32[3072,256]{1,0:T(8,128)} %gather_fusion.6), kind=kLoop, calls=%fused_computation.29 | loop fusion | flops 1572864 | bytes 12585984 | tf_op jit(solution)/shard_map/jit(_take)/select_n | solution.py:83
  202.8 4.3 %all-to-all-done.2 = f32[128,1,128]{2,1,0:T(1,128)S(1)} async-done(((f32[128,1,128]{2,1,0:T(1,128)}), f32[128,1,128]{2,1,0:T(1,128)S(1)}, u32[]{:S(2)}, u32[]{:S(2)}) %all-to-all-start.2) | async-done | bytes 65568 | tf_op jit(solution)/shard_map/all_to_all | solution.py:93
  207.1 46.6 %all_to_all.60 = f32[128,24,256]{2,1,0:T(8,128)} all-to-all(f32[128,24,256]{2,1,0:T(8,128)} %bitcast.87), channel_id=1, replica_groups=mesh['expo'=8,'sky'=16] {'expo','sky'}, dimensions={0} | all-to-all | bytes 6291456 | tf_op jit(solution)/shard_map/all_to_all | solution.py:84
  253.6 5.1 %all-to-all-start.4 = ((f32[128,24,256]{2,1,0:T(8,128)}), f32[128,24,256]{2,1,0:T(8,128)}, u32[]{:S(2)}, u32[]{:S(2)}) async-start(f32[128,24,256]{2,1,0:T(8,128)} %bitcast.85), calls=%async_computation.4 | async-start | bytes 6291456 | tf_op jit(solution)/shard_map/all_to_all | solution.py:84
  258.8 0.1 copy.26
  258.9 0.1 eq.26
  259.0 0.3 fusion.14
  259.3 0.6 mul.149
  259.9 0.4 copy.34
  260.3 0.1 mul.152
  260.5 0.9 mul.153
  261.3 0.3 reshape.287
  261.6 1.6 fusion.15
  263.2 3.6 %fusion.8 = f32[64,2,256]{2,0,1:T(8,128)S(1)} fusion(f32[3072,256,1]{1,0,2:T(8,128)} %bitcast.86, f32[2,3072]{1,0:T(2,128)S(1)} %mul.153, f32[64,3072]{1,0:T(8,128)S(1)} %copy.34), kind=kOutput, calls=%fused_computation.26 | convolution fusion | flops 1208352768 | bytes 4087808 | tf_op jit(solution)/shard_map/dot_general | solution.py:85
  266.7 32.8 %all-to-all-done.4 = f32[128,24,256]{2,1,0:T(8,128)} async-done(((f32[128,24,256]{2,1,0:T(8,128)}), f32[128,24,256]{2,1,0:T(8,128)}, u32[]{:S(2)}, u32[]{:S(2)}) %all-to-all-start.4) | async-done | bytes 3145760 | tf_op jit(solution)/shard_map/all_to_all | solution.py:84
  299.6 3.6 %fusion.6 = f32[64,2,256]{2,0,1:T(8,128)S(1)} fusion(f32[3072,256,1]{1,0,2:T(8,128)} %bitcast.24, f32[2,3072]{1,0:T(2,128)S(1)} %mul.153, f32[64,3072]{1,0:T(8,128)S(1)} %copy.34), kind=kOutput, calls=%fused_computation.24 | convolution fusion | flops 1208352768 | bytes 4087808 | tf_op jit(solution)/shard_map/dot_general | solution.py:85
  303.2 0.9 copy.35
  (23 shorter events, 0.1 us)
Async XLA Ops:
  0.6 95.7 %copy-start = (bf16[256,1024]{1,0:T(8,128)(2,1)S(1)}, bf16[256,1024]{1,0:T(8,128)(2,1)}, u32[]{:S(2)}) copy-start(bf16[256,1024]{1,0:T(8,128)(2,1)} %param.10) | copy-start | bytes 1572868
  19.9 19.7 %copy-start.3 = (s32[8,16]{1,0:T(8,128)S(1)}, s32[8,16]{1,0:T(8,128)}, u32[]{:S(2)}) copy-start(s32[8,16]{1,0:T(8,128)} %param.15) | copy-start | bytes 1540
  32.9 30.0 %all-to-all-start.1 = ((bf16[16,192,256]{2,1,0:T(8,128)(2,1)}), bf16[16,192,256]{2,1,0:T(8,128)(2,1)S(1)}, u32[]{:S(2)}, u32[]{:S(2)}) async-start(bf16[16,192,256]{2,1,0:T(8,128)(2,1)} %bitcast.89), calls=%async_computation.1 | async-start | bytes 3145728 | tf_op jit(solution)/shard_map/all_to_all | solution.py:60
  62.9 25.2 %all-to-all-start = ((bf16[16,192,256]{2,1,0:T(8,128)(2,1)}), bf16[16,192,256]{2,1,0:T(8,128)(2,1)}, u32[]{:S(2)}, u32[]{:S(2)}) async-start(bf16[16,192,256]{2,1,0:T(8,128)(2,1)} %bitcast.88), calls=%async_computation | async-start | bytes 3145728 | tf_op jit(solution)/shard_map/all_to_all | solution.py:60
  100.8 12.7 %copy-start.1 = (f32[8,16,1024]{2,1,0:T(8,128)S(1)}, f32[8,16,1024]{2,1,0:T(8,128)}, u32[]{:S(2)}) copy-start(f32[8,16,1024]{2,1,0:T(8,128)} %param.12) | copy-start | bytes 1572868
  100.8 12.7 %copy-start.2 = (f32[8,16,1024]{2,1,0:T(8,128)S(1)}, f32[8,16,1024]{2,1,0:T(8,128)}, u32[]{:S(2)}) copy-start(f32[8,16,1024]{2,1,0:T(8,128)} %param.13) | copy-start | bytes 1572868
  188.7 18.3 %all-to-all-start.2 = ((f32[128,1,128]{2,1,0:T(1,128)}), f32[128,1,128]{2,1,0:T(1,128)S(1)}, u32[]{:S(2)}, u32[]{:S(2)}) async-start(f32[128,1,128]{2,1,0:T(1,128)} %bitcast.14), calls=%async_computation.2 | async-start | bytes 131072 | tf_op jit(solution)/shard_map/all_to_all | solution.py:93
  253.6 45.9 %all-to-all-start.4 = ((f32[128,24,256]{2,1,0:T(8,128)}), f32[128,24,256]{2,1,0:T(8,128)}, u32[]{:S(2)}, u32[]{:S(2)}) async-start(f32[128,24,256]{2,1,0:T(8,128)} %bitcast.85), calls=%async_computation.4 | async-start | bytes 6291456 | tf_op jit(solution)/shard_map/all_to_all | solution.py:84
